TPU v7x, 256 devices: a whole 4x4x8 slice. The times are simulated.
256 devices in a mesh: dp: 8 (over z_hi, x), ctx: 32 (over y, z_lo, core).
Axes of the slice: x: 4, y: 4, z: 8 (z_hi: 2, z_lo: 4; z = z_hi * 4 + z_lo), core: 2. Of those that a mesh axis runs over, the one named last changes fastest.
Arguments:
- y_first: bfloat16 [8, 4096, 1024], P('dp', 'ctx'), may hold values from -6 to 6
- x_second: bfloat16 [8, 4096, 1024], P('dp', 'ctx'), may hold values from -40 to 40
- grad_first: bfloat16 [8, 4096, 1024], P('dp', 'ctx'), may hold values from -6 to 6
- grad_second: bfloat16 [8, 4096, 1024], P('dp', 'ctx'), may hold values from -6 to 6
- w_query: bfloat16 [1024, 1024], P('dp'), may hold values from -0.1875 to 0.1875
- w_key: bfloat16 [1024, 1024], P('dp'), may hold values from -0.1875 to 0.1875
- w_value: bfloat16 [1024, 1024], P('dp'), may hold values from -0.1875 to 0.1875
- w_out: bfloat16 [1024, 1024], P('dp'), may hold values from -0.1875 to 0.1875
Outputs:
- x_first: bfloat16 [8, 4096, 1024], P('dp', 'ctx')
- grad_x_second: bfloat16 [8, 4096, 1024], P('dp', 'ctx')
- grad_query: float32 [1024, 1024], P(('dp', 'ctx'))
- grad_out: float32 [1024, 1024], P(('dp', 'ctx'))
All inputs are finite; a program needn't handle non-finite values.
Results may differ from a plain program's by a relative error of at most 0.012.
The roundings to bfloat16 on the way count: a program that leaves them out, or rounds other values in their place, can miss the bound.
Values may be sent and summed in bfloat16 or wider, within the bound.
No kernel may reach another device: no remote copies, remote signals or barrier semaphores. Data moves between devices by JAX's collectives and lax.ppermute only.
A program may use at most 128 MiB of HBM per device.

v0:
```python
import jax
import jax.numpy as jnp
from jax import lax
from jax.sharding import PartitionSpec as P

HEADS = 8
HEAD_DIM = 128


def scan_sum(shard, axis, reverse):
    count = lax.axis_size(axis)
    total = shard
    step = 1
    while step < count:
        if reverse:
            pairs = [(source, source - step) for source in range(step, count)]
        else:
            pairs = [(source, source + step) for source in range(count - step)]
        total = total + lax.ppermute(total, axis, pairs)
        step *= 2
    return total


def gather_rows(weights, piece):
    place = lax.axis_index("ctx")
    parts = [lax.dynamic_slice_in_dim(weight, place * piece, piece, 0) for weight in weights]
    joined = jnp.concatenate(parts, 0)
    gathered = lax.all_gather(joined, ("dp", "ctx"), axis=0, tiled=True)
    gathered = gathered.reshape(-1, len(weights), piece, joined.shape[1])
    return tuple((gathered[:, index].reshape(-1, joined.shape[1]) for index in range(len(weights))))


def weight_grads(pairs, factor, owners):
    width = pairs[0][0].shape[1]
    blocks = []
    for left, right in pairs:
        made = lax.dot_general(
            left, right, (((0,), (0,)), ((), ())), preferred_element_type=jnp.float32
        )
        blocks.append((factor * made).reshape(owners, -1, width))
    rows = blocks[0].shape[1]
    stacked = jnp.concatenate(blocks, 1).reshape(-1, width)
    share = lax.psum_scatter(stacked, ("dp", "ctx"), scatter_dimension=0, tiled=True)
    return tuple((share[index * rows : (index + 1) * rows] for index in range(len(pairs))))


def on_device(y_first, x_second, grad_first, grad_second, w_query, w_key, w_value, w_out):
    batch, tokens_here, width = y_first.shape
    owners = lax.axis_size("dp") * lax.axis_size("ctx")
    factor = float(batch * tokens_here * owners) ** (-0.5)
    piece = w_query.shape[0] // lax.axis_size("ctx")
    full_query, full_key, full_value = gather_rows((w_query, w_key, w_value), piece)
    (full_out,) = gather_rows((w_out,), piece)
    second_wide = x_second.astype(jnp.float32)
    inv_rms = lax.rsqrt(jnp.mean(second_wide * second_wide, -1, keepdims=True) + 1e-06)
    normed_wide = second_wide * inv_rms
    normed = normed_wide.astype(jnp.bfloat16)

    def project(weight):
        made = jnp.einsum("btd,df->btf", normed, weight, preferred_element_type=jnp.float32)
        return made.astype(jnp.bfloat16).reshape(batch, tokens_here, HEADS, HEAD_DIM)

    queries = project(full_query)
    key_rows = project(full_key)
    values = project(full_value)
    local_state = jnp.einsum(
        "bthe,bthf->bhef", key_rows, values, preferred_element_type=jnp.float32
    )
    before = (scan_sum(local_state, "ctx", False) - local_state).astype(jnp.bfloat16)
    causal = jnp.tril(jnp.ones((tokens_here, tokens_here), dtype=bool))
    scores = jnp.einsum("bthe,bshe->bhts", queries, key_rows, preferred_element_type=jnp.float32)
    scores = jnp.where(causal[None, None], scores, 0.0).astype(jnp.bfloat16)
    mixed = jnp.einsum("bhts,bshf->bthf", scores, values, preferred_element_type=jnp.float32)
    mixed = mixed + jnp.einsum(
        "bthe,bhef->bthf", queries, before, preferred_element_type=jnp.float32
    )
    inv_head = lax.rsqrt(jnp.mean(mixed * mixed, -1, keepdims=True) + 1e-06)
    unit = mixed * inv_head
    attn_out = unit.astype(jnp.bfloat16).reshape(batch, tokens_here, width)
    attended = jnp.einsum("btf,fd->btd", attn_out, full_out, preferred_element_type=jnp.float32)
    x_first = (y_first.astype(jnp.float32) - attended).astype(jnp.bfloat16)
    grad_unit = jnp.einsum("btd,fd->btf", grad_first, full_out, preferred_element_type=jnp.float32)
    grad_unit = grad_unit.reshape(batch, tokens_here, HEADS, HEAD_DIM)
    grad_mixed = inv_head * (grad_unit - unit * jnp.mean(grad_unit * unit, -1, keepdims=True))
    grad_mixed = grad_mixed.astype(jnp.bfloat16)
    score_grad = jnp.einsum(
        "bthf,bshf->bhts", grad_mixed, values, preferred_element_type=jnp.float32
    )
    score_grad = jnp.where(causal[None, None], score_grad, 0.0).astype(jnp.bfloat16)
    grad_local = jnp.einsum(
        "bthe,bthf->bhef", queries, grad_mixed, preferred_element_type=jnp.float32
    )
    after_state = (scan_sum(grad_local, "ctx", True) - grad_local).astype(jnp.bfloat16)
    query_grad = jnp.einsum(
        "bhts,bshe->bthe", score_grad, key_rows, preferred_element_type=jnp.float32
    )
    query_grad = query_grad + jnp.einsum(
        "bthf,bhef->bthe", grad_mixed, before, preferred_element_type=jnp.float32
    )
    key_grad = jnp.einsum(
        "bhts,bthe->bshe", score_grad, queries, preferred_element_type=jnp.float32
    )
    key_grad = key_grad + jnp.einsum(
        "bshf,bhef->bshe", values, after_state, preferred_element_type=jnp.float32
    )
    value_grad = jnp.einsum(
        "bhts,bthf->bshf", scores, grad_mixed, preferred_element_type=jnp.float32
    )
    value_grad = value_grad + jnp.einsum(
        "bshe,bhef->bshf", key_rows, after_state, preferred_element_type=jnp.float32
    )
    query_grad = query_grad.astype(jnp.bfloat16).reshape(batch, tokens_here, width)
    key_grad = key_grad.astype(jnp.bfloat16).reshape(batch, tokens_here, width)
    value_grad = value_grad.astype(jnp.bfloat16).reshape(batch, tokens_here, width)
    grad_normed = jnp.einsum(
        "btf,df->btd", query_grad, full_query, preferred_element_type=jnp.float32
    )
    grad_normed = grad_normed + jnp.einsum(
        "btf,df->btd", key_grad, full_key, preferred_element_type=jnp.float32
    )
    grad_normed = grad_normed + jnp.einsum(
        "btf,df->btd", value_grad, full_value, preferred_element_type=jnp.float32
    )
    back = inv_rms * (
        grad_normed - normed_wide * jnp.mean(grad_normed * normed_wide, -1, keepdims=True)
    )
    grad_x_second = (grad_second.astype(jnp.float32) + back).astype(jnp.bfloat16)
    pairs = (
        (normed.reshape(-1, width), query_grad.reshape(-1, width)),
        (attn_out.reshape(-1, width), grad_first.reshape(-1, width)),
    )
    grad_query, grad_out = weight_grads(pairs, factor, owners)
    return (x_first, grad_x_second, grad_query, grad_out)


def solution(mesh):
    placed = (
        P("dp", "ctx", None),
        P("dp", "ctx", None),
        P("dp", "ctx", None),
        P("dp", "ctx", None),
        P("dp", None),
        P("dp", None),
        P("dp", None),
        P("dp", None),
    )
    return jax.shard_map(
        on_device,
        mesh=mesh,
        in_specs=placed,
        out_specs=(
            P("dp", "ctx", None),
            P("dp", "ctx", None),
            P(("dp", "ctx"), None),
            P(("dp", "ctx"), None),
        ),
        check_vma=False,
    )
```

profile of v0, /device:TPU:0, one launch (start us, length us, event | category | flops | bytes accessed | tf_op | source)
XLA Modules:
  0.0 2217.5 jit_solution(11344175683100216950)
XLA Ops:
  11.9 420.7 %all-gather.5.cloned.1.call-done = bf16[256,12,1024]{2,1,0:T(8,128)(2,1)} async-done(((bf16[1,12,1024]{2,1,0:T(8,128)(2,1)}), bf16[256,12,1024]{2,1,0:T(8,128)(2,1)}) %all-gather.5.cloned.1.call-update) | async-done | bytes 6291472 | tf_op jit(solution)/shard_map/all_gather | solution.py:28
  432.6 6.9 copy.67
  439.5 3.4 fusion.43
  442.9 2.9 copy.68
  445.9 2.5 reshape_squeeze.9
  448.4 4.5 copy.70
  452.9 4.0 reshape_squeeze.11
  457.0 2.1 convolution_convert_fusion
  463.7 10.4 collective-permute-start.1
  474.1 10.7 collective-permute-done.1
  484.8 4.5 collective-permute-start.2
  489.4 9.0 collective-permute-done.2
  499.2 16.1 collective-permute-start.3
  515.4 342.0 %all-gather.7.cloned.1.call-done = bf16[256,4,1024]{2,1,0:T(4,128)(2,1)} async-done(((bf16[1,4,1024]{2,1,0:T(4,128)(2,1)}), bf16[256,4,1024]{2,1,0:T(4,128)(2,1)}) %all-gather.7.cloned.1.call-update) | async-done | bytes 2097168 | tf_op jit(solution)/shard_map/all_gather | solution.py:28
  857.4 4.0 reshape.224
  861.4 3.3 fusion.31
  864.7 3.0 copy.69
  867.7 4.0 reshape_squeeze.10
  871.7 2.0 add.103
  873.7 2.1 collective-permute-start.4
  875.8 2.8 convolution_convert_fusion.1
  888.6 2.8 convolution_multiply_fusion.1
  891.4 5.2 reshape.218
  896.6 3.6 convolution_multiply_fusion
  900.2 5.2 reshape.219
  905.4 8.9 maximum_bitcast_fusion
  916.0 2.5 collective-permute-done.5
  920.0 18.2 collective-permute-done.6
  939.6 31.6 %collective-permute-done.7 = f32[1,8,128,128]{3,2,1,0:T(8,128)S(1)} collective-permute-done((f32[1,8,128,128]{3,2,1,0:T(8,128)S(1)}, f32[1,8,128,128]{3,2,1,0:T(8,128)S(1)}, u32[]{:S(2)}, u32[]{:S(2)}) %collective-permute-start.7) | collective-permute-done | bytes 524320 | tf_op jit(solution)/shard_map/ppermute | solution.py:19
  973.7 12.9 collective-permute-done.8
  989.6 15.4 collective-permute-done.9
  1008.5 1201.0 %reduce-scatter.2.cloned.1.call-done = f32[8,1024]{1,0:T(8,128)} async-done(((f32[2048,1024]{1,0:T(8,128)}), f32[8,1024]{1,0:T(8,128)}) %reduce-scatter.2.cloned.1.call-update) | async-done | bytes 32784 | tf_op jit(solution)/shard_map/reduce_scatter | solution.py:43
  (102 shorter events, 35.1 us)
Async XLA Ops:
  7.2 854.2 %copy-start = (bf16[1,128,1024]{2,1,0:T(8,128)(2,1)S(1)}, bf16[1,128,1024]{2,1,0:T(8,128)(2,1)}, u32[]{:S(2)}) copy-start(bf16[1,128,1024]{2,1,0:T(8,128)(2,1)} %param.10) | copy-start | bytes 786436
  7.2 425.5 %all-gather.5.cloned.1.call-start = ((), (), s32[]{:S(2)}) async-start(), calls=%async_computation.2 | async-start | bytes 8421376 | tf_op jit(solution)/shard_map/all_gather | solution.py:28
  9.4 848.0 %all-gather.7.cloned.1.call-start = ((), (), s32[]{:S(2)}) async-start(), calls=%async_computation.3 | async-start | bytes 2105344 | tf_op jit(solution)/shard_map/all_gather | solution.py:28
  10.8 2198.7 %reduce-scatter.2.cloned.1.call-start = ((), (), s32[]{:S(2)}) async-start(), calls=%async_computation.1 | async-start | bytes 8421376 | tf_op jit(solution)/shard_map/reduce_scatter | solution.py:43
  452.9 4.0 copy-start.4
  460.1 3.6 copy-start.13
  460.6 24.3 %copy-start.7 = (bf16[16,8,8,128]{3,2,1,0:T(8,128)(2,1)}, bf16[16,8,8,128]{3,2,1,0:T(8,128)(2,1)S(1)}, u32[]{:S(2)}) copy-start(bf16[16,8,8,128]{3,2,1,0:T(8,128)(2,1)S(1)} %fusion.9) | copy-start | bytes 786436
  460.8 2.8 collective-permute-start
  463.7 21.1 collective-permute-start.1
  484.8 13.5 collective-permute-start.2
  499.2 372.4 %collective-permute-start.3 = (f32[1,8,128,128]{3,2,1,0:T(8,128)}, f32[1,8,128,128]{3,2,1,0:T(8,128)}, u32[]{:S(2)}, u32[]{:S(2)}) collective-permute-start(f32[1,8,128,128]{3,2,1,0:T(8,128)} %add.102), channel_id=1, source_target_pairs={{0,8},{1,9},{2,10},{3,11},{4,12},{5,13},{6,14},{7,15},{8,16},{9,17... | collective-permute-start | bytes 1572872 | tf_op jit(solution)/shard_map/ppermute | solution.py:19
  861.4 3.3 copy-start.5
  873.7 10.6 collective-permute-start.4
  881.0 1.4 copy-start.16
  881.0 5.0 copy-start.6
  885.6 1.3 copy-start.8
  885.9 1.3 copy-start.14
  914.6 58.0 %copy-start.19 = (bf16[8,128,128]{2,1,0:T(8,128)(2,1)S(1)}, bf16[8,128,128]{2,1,0:T(8,128)(2,1)}, u32[]{:S(2)}) copy-start(bf16[8,128,128]{2,1,0:T(8,128)(2,1)} %copy-done.18) | copy-start | bytes 786436
  914.6 3.9 collective-permute-start.5
  918.6 54.2 %copy-start.2 = (bf16[1024,1024]{1,0:T(8,128)(2,1)S(1)}, bf16[1024,1024]{1,0:T(8,128)(2,1)}, u32[]{:S(2)}) copy-start(bf16[1024,1024]{1,0:T(8,128)(2,1)} %reshape_squeeze.10) | copy-start | bytes 6291460
  918.6 54.2 %copy-start.10 = (bf16[8,128,128]{2,1,0:T(8,128)(2,1)S(1)}, bf16[8,128,128]{2,1,0:T(8,128)(2,1)}, u32[]{:S(2)}) copy-start(bf16[8,128,128]{2,1,0:T(8,128)(2,1)} %copy-done.9) | copy-start | bytes 786436
  918.6 19.6 collective-permute-start.6
  938.3 32.9 %collective-permute-start.7 = (f32[1,8,128,128]{3,2,1,0:T(8,128)S(1)}, f32[1,8,128,128]{3,2,1,0:T(8,128)S(1)}, u32[]{:S(2)}, u32[]{:S(2)}) collective-permute-start(f32[1,8,128,128]{3,2,1,0:T(8,128)S(1)} %add.112), channel_id=1, source_target_pairs={{4,0},{5,1},{6,2},{7,3},{8,4},{9,5},{10,6},{11,7},{12,8},{13,9},{1... | collective-permute-start | bytes 1572872 | tf_op jit(solution)/shard_map/ppermute | solution.py:19
  971.2 15.3 collective-permute-start.8
  972.8 15.4 copy-start.17
  972.8 15.6 copy-start.1
  972.8 15.6 copy-start.15
  972.8 15.6 copy-start.21
  986.6 18.4 collective-permute-start.9
  988.4 16.7 copy-start.12
  989.6 16.2 copy-start.3
  1006.6 1.0 copy-start.20
  (3 other events, 2.1 us)
Sparse Core Ops, SparseCore 0:
  10.4 422.1 all-gather.4
  435.1 422.2 all-gather.6
  914.4 1295.0 reduce-scatter.1
where the time goes:
time: 2220 us
  waiting for transfers between devices  2070 us (93%)
  local copies, waits for them, and re-layouts  53 us (2%)
  starting transfers between devices  41.5 us (2%)
  matrix products  24.2 us (1%)
    reduce_scatter x1, waiting for transfers between devices, weight_grads(): lax.psum_scatter(stacked, ('dp', 'ctx'), scatter_dimension=0, tiled=True)  1200 us
    all_gather x2, waiting for transfers between devices, gather_rows(): gathered = lax.all_gather(joined, ('dp', 'ctx'), axis=0, tiled=True)  763 us
    ppermute x10, waiting for transfers between devices, scan_sum(): total = total + lax.ppermute(total, axis, pairs)  104 us
  transfers between devices with their start and end apart: 13, of which 12 were waited for; matrix products, arithmetic and copies ran while one was open for 3% of the time, Pallas kernels for 0%

commit v1 on v0

--- a/solution.py
+++ b/solution.py
@@ -25,7 +25,10 @@
     place = lax.axis_index("ctx")
     parts = [lax.dynamic_slice_in_dim(weight, place * piece, piece, 0) for weight in weights]
     joined = jnp.concatenate(parts, 0)
-    gathered = lax.all_gather(joined, ("dp", "ctx"), axis=0, tiled=True)
+    gathered = jnp.concatenate(
+        lax.all_to_all(jnp.stack([joined] * lax.axis_size(("dp", "ctx"))), ("dp", "ctx"), 0, 0),
+        axis=0,
+    )
     gathered = gathered.reshape(-1, len(weights), piece, joined.shape[1])
     return tuple((gathered[:, index].reshape(-1, joined.shape[1]) for index in range(len(weights))))
 

time: 2220 us -> 1690 us (0.76)
  waiting for transfers between devices: 2070 us -> 1490 us
  starting transfers between devices: 41.5 us -> 85.3 us
    all_gather x2 -> x0, waiting for transfers between devices: 763 us -> none  [gather_rows(): gathered = lax.all_gather(joined, ('dp', 'ctx'), axis=0, tiled=True)]
    all_to_all x0 -> x2, waiting for transfers between devices: none -> 183 us  [gather_rows(): lax.all_to_all(jnp.stack([joined] * lax.axis_size(('dp', 'ctx'))), ('dp',...]
    all_to_all x0 -> x2, starting transfers between devices: none -> 26.7 us  [gather_rows(): lax.all_to_all(jnp.stack([joined] * lax.axis_size(('dp', 'ctx'))), ('dp',...]
  transfers between devices with their start and end apart: 13 -> 13, of which waited for: 12 -> 11; matrix products, arithmetic and copies ran while one was open for 3% -> 3% of each run, Pallas kernels for 0% -> 0%
where the time goes in v1:
time: 1690 us
  waiting for transfers between devices  1490 us (88%)
  starting transfers between devices  85.3 us (5%)
  local copies, waits for them, and re-layouts  54.6 us (3%)
  matrix products  24.9 us (1%)
    reduce_scatter x1, waiting for transfers between devices, weight_grads(): lax.psum_scatter(stacked, ('dp', 'ctx'), scatter_dimension=0, tiled=True)  1210 us
    all_to_all x2, waiting for transfers between devices, gather_rows(): lax.all_to_all(jnp.stack([joined] * lax.axis_size(('dp', 'ctx'))), ('dp',...  183 us
    ppermute x10, waiting for transfers between devices, scan_sum(): total = total + lax.ppermute(total, axis, pairs)  105 us
    ppermute x10, starting transfers between devices, scan_sum(): total = total + lax.ppermute(total, axis, pairs)  58.3 us
  transfers between devices with their start and end apart: 13, of which 11 were waited for; matrix products, arithmetic and copies ran while one was open for 3% of the time, Pallas kernels for 0%

profile of v1, /device:TPU:0, one launch (start us, length us, event | category | flops | bytes accessed | tf_op | source)
XLA Modules:
  0.0 1687.3 jit_solution(5650302011925631575)
XLA Ops:
  8.7 4.3 stack.4
  13.0 15.7 all-to-all-start
  29.4 182.7 %all-to-all-done = bf16[256,12,1024]{2,1,0:T(8,128)(2,1)} async-done(((bf16[256,12,1024]{2,1,0:T(8,128)(2,1)}), bf16[256,12,1024]{2,1,0:T(8,128)(2,1)}, u32[]{:S(2)}, u32[]{:S(2)}) %all-to-all-start) | async-done | bytes 6291488 | tf_op jit(solution)/shard_map/all_to_all | solution.py:29
  214.0 11.0 all-to-all-start.1
  225.5 6.9 copy.66
  232.4 3.1 fusion.43
  239.2 4.6 copy.67
  243.7 2.5 reshape_squeeze.9
  246.3 2.1 convolution_convert_fusion
  253.0 23.2 %collective-permute-start.1 = (f32[1,8,128,128]{3,2,1,0:T(8,128)S(1)}, f32[1,8,128,128]{3,2,1,0:T(8,128)S(1)}, u32[]{:S(2)}, u32[]{:S(2)}) collective-permute-start(f32[1,8,128,128]{3,2,1,0:T(8,128)S(1)} %add.100), channel_id=1, source_target_pairs={{0,2},{1,3},{2,4},{3,5},{4,6},{5,7},{6,8},{7,9},{8,10},{9,11},{10,... | collective-permute-start | bytes 1572872 | tf_op jit(solution)/shard_map/ppermute | solution.py:19
  276.2 10.5 collective-permute-done.1
  286.7 5.4 collective-permute-start.2
  292.2 9.8 collective-permute-done.2
  302.8 16.3 collective-permute-start.3
  319.2 4.0 reshape_squeeze_reshape_reshape.3
  323.2 3.3 fusion.31
  326.5 3.0 copy.68
  329.5 4.0 reshape_squeeze.10
  335.5 5.1 collective-permute-start.4
  340.6 2.8 convolution_convert_fusion.1
  347.2 2.2 collective-permute-done.4
  353.3 2.6 convolution_multiply_fusion
  355.9 5.2 reshape.219
  361.1 3.7 convolution_multiply_fusion.1
  364.8 5.2 reshape.218
  370.0 8.9 maximum_bitcast_fusion
  380.7 2.5 collective-permute-done.5
  384.7 19.0 %collective-permute-done.6 = f32[1,8,128,128]{3,2,1,0:T(8,128)S(1)} collective-permute-done((f32[1,8,128,128]{3,2,1,0:T(8,128)S(1)}, f32[1,8,128,128]{3,2,1,0:T(8,128)S(1)}, u32[]{:S(2)}, u32[]{:S(2)}) %collective-permute-start.6) | collective-permute-done | bytes 524320 | tf_op jit(solution)/shard_map/ppermute | solution.py:19
  405.1 28.3 %collective-permute-done.7 = f32[1,8,128,128]{3,2,1,0:T(8,128)S(1)} collective-permute-done((f32[1,8,128,128]{3,2,1,0:T(8,128)S(1)}, f32[1,8,128,128]{3,2,1,0:T(8,128)S(1)}, u32[]{:S(2)}, u32[]{:S(2)}) %collective-permute-start.7) | collective-permute-done | bytes 524320 | tf_op jit(solution)/shard_map/ppermute | solution.py:19
  435.9 15.9 collective-permute-done.8
  454.8 15.0 collective-permute-done.9
  473.3 1205.7 %reduce-scatter.2.cloned.1.call-done = f32[8,1024]{1,0:T(8,128)} async-done(((f32[2048,1024]{1,0:T(8,128)}), f32[8,1024]{1,0:T(8,128)}) %reduce-scatter.2.cloned.1.call-update) | async-done | bytes 32784 | tf_op jit(solution)/shard_map/reduce_scatter | solution.py:46
  (102 shorter events, 38.2 us)
Async XLA Ops:
  7.2 316.0 %copy-start = (bf16[1,128,1024]{2,1,0:T(8,128)(2,1)S(1)}, bf16[1,128,1024]{2,1,0:T(8,128)(2,1)}, u32[]{:S(2)}) copy-start(bf16[1,128,1024]{2,1,0:T(8,128)(2,1)} %param.10) | copy-start | bytes 786436
  13.0 199.1 %all-to-all-start = ((bf16[256,12,1024]{2,1,0:T(8,128)(2,1)}), bf16[256,12,1024]{2,1,0:T(8,128)(2,1)}, u32[]{:S(2)}, u32[]{:S(2)}) async-start(bf16[256,12,1024]{2,1,0:T(8,128)(2,1)} %stack.4), calls=%async_computation | async-start | bytes 16777216 | tf_op jit(solution)/shard_map/all_to_all | solution.py:29
  214.0 11.3 copy-start.4
  214.0 105.2 %all-to-all-start.1 = ((bf16[256,4,1024]{2,1,0:T(4,128)(2,1)}), bf16[256,4,1024]{2,1,0:T(4,128)(2,1)}, u32[]{:S(2)}, u32[]{:S(2)}) async-start(bf16[256,4,1024]{2,1,0:T(4,128)(2,1)} %stack.5), calls=%async_computation.1 | async-start | bytes 4194304 | tf_op jit(solution)/shard_map/all_to_all | solution.py:29
  225.1 1454.0 %reduce-scatter.2.cloned.1.call-start = ((), (), s32[]{:S(2)}) async-start(), calls=%async_computation.3 | async-start | bytes 8421376 | tf_op jit(solution)/shard_map/reduce_scatter | solution.py:46
  249.3 3.6 copy-start.12
  249.9 36.9 %copy-start.7 = (bf16[16,8,8,128]{3,2,1,0:T(8,128)(2,1)}, bf16[16,8,8,128]{3,2,1,0:T(8,128)(2,1)S(1)}, u32[]{:S(2)}) copy-start(bf16[16,8,8,128]{3,2,1,0:T(8,128)(2,1)S(1)} %fusion.9) | copy-start | bytes 786436
  250.1 2.8 collective-permute-start
  253.0 33.7 %collective-permute-start.1 = (f32[1,8,128,128]{3,2,1,0:T(8,128)S(1)}, f32[1,8,128,128]{3,2,1,0:T(8,128)S(1)}, u32[]{:S(2)}, u32[]{:S(2)}) collective-permute-start(f32[1,8,128,128]{3,2,1,0:T(8,128)S(1)} %add.100), channel_id=1, source_target_pairs={{0,2},{1,3},{2,4},{3,5},{4,6},{5,7},{6,8},{7,9},{8,10},{9,11},{10,... | collective-permute-start | bytes 1572872 | tf_op jit(solution)/shard_map/ppermute | solution.py:19
  286.7 15.3 collective-permute-start.2
  302.8 30.7 %collective-permute-start.3 = (f32[1,8,128,128]{3,2,1,0:T(8,128)}, f32[1,8,128,128]{3,2,1,0:T(8,128)}, u32[]{:S(2)}, u32[]{:S(2)}) collective-permute-start(f32[1,8,128,128]{3,2,1,0:T(8,128)} %add.102), channel_id=1, source_target_pairs={{0,8},{1,9},{2,10},{3,11},{4,12},{5,13},{6,14},{7,15},{8,16},{9,17... | collective-permute-start | bytes 1572872 | tf_op jit(solution)/shard_map/ppermute | solution.py:19
  323.2 3.3 copy-start.5
  335.5 13.9 collective-permute-start.4
  345.8 1.4 copy-start.16
  345.8 5.2 copy-start.6
  351.0 1.0 copy-start.13
  351.3 2.0 copy-start.14
  352.0 1.3 copy-start.18
  379.2 55.5 %copy-start.19 = (bf16[8,128,128]{2,1,0:T(8,128)(2,1)S(1)}, bf16[8,128,128]{2,1,0:T(8,128)(2,1)}, u32[]{:S(2)}) copy-start(bf16[8,128,128]{2,1,0:T(8,128)(2,1)} %copy-done.18) | copy-start | bytes 786436
  379.3 3.9 collective-permute-start.5
  383.2 51.7 %copy-start.2 = (bf16[1024,1024]{1,0:T(8,128)(2,1)S(1)}, bf16[1024,1024]{1,0:T(8,128)(2,1)}, u32[]{:S(2)}) copy-start(bf16[1024,1024]{1,0:T(8,128)(2,1)} %reshape_squeeze.10) | copy-start | bytes 6291460
  383.3 51.7 %copy-start.9 = (bf16[8,128,128]{2,1,0:T(8,128)(2,1)S(1)}, bf16[8,128,128]{2,1,0:T(8,128)(2,1)}, u32[]{:S(2)}) copy-start(bf16[8,128,128]{2,1,0:T(8,128)(2,1)} %fusion.6) | copy-start | bytes 786436
  383.3 20.5 %collective-permute-start.6 = (f32[1,8,128,128]{3,2,1,0:T(8,128)S(1)}, f32[1,8,128,128]{3,2,1,0:T(8,128)S(1)}, u32[]{:S(2)}, u32[]{:S(2)}) collective-permute-start(f32[1,8,128,128]{3,2,1,0:T(8,128)S(1)} %add.111), channel_id=1, source_target_pairs={{2,0},{3,1},{4,2},{5,3},{6,4},{7,5},{8,6},{9,7},{10,8},{11,9},{12,... | collective-permute-start | bytes 1572872 | tf_op jit(solution)/shard_map/ppermute | solution.py:19
  403.8 29.6 %collective-permute-start.7 = (f32[1,8,128,128]{3,2,1,0:T(8,128)S(1)}, f32[1,8,128,128]{3,2,1,0:T(8,128)S(1)}, u32[]{:S(2)}, u32[]{:S(2)}) collective-permute-start(f32[1,8,128,128]{3,2,1,0:T(8,128)S(1)} %add.112), channel_id=1, source_target_pairs={{4,0},{5,1},{6,2},{7,3},{8,4},{9,5},{10,6},{11,7},{12,8},{13,9},{1... | collective-permute-start | bytes 1572872 | tf_op jit(solution)/shard_map/ppermute | solution.py:19
  433.4 18.3 %collective-permute-start.8 = (f32[1,8,128,128]{3,2,1,0:T(8,128)S(1)}, f32[1,8,128,128]{3,2,1,0:T(8,128)S(1)}, u32[]{:S(2)}, u32[]{:S(2)}) collective-permute-start(f32[1,8,128,128]{3,2,1,0:T(8,128)S(1)} %add.113), channel_id=1, source_target_pairs={{8,0},{9,1},{10,2},{11,3},{12,4},{13,5},{14,6},{15,7},{16,8},{17,9... | collective-permute-start | bytes 1572872 | tf_op jit(solution)/shard_map/ppermute | solution.py:19
  435.0 18.4 %copy-start.17 = (bf16[8,128,128]{2,1,0:T(8,128)(2,1)S(1)}, bf16[8,128,128]{2,1,0:T(8,128)(2,1)}, u32[]{:S(2)}) copy-start(bf16[8,128,128]{2,1,0:T(8,128)(2,1)} %copy-done.16) | copy-start | bytes 786436
  435.0 18.6 %copy-start.1 = (bf16[1024,1024]{1,0:T(8,128)(2,1)S(1)}, bf16[1024,1024]{1,0:T(8,128)(2,1)}, u32[]{:S(2)}) copy-start(bf16[1024,1024]{1,0:T(8,128)(2,1)} %reshape_squeeze_reshape_reshape.3) | copy-start | bytes 6291460
  435.0 18.6 %copy-start.15 = (bf16[1,128,8,128]{1,3,2,0:T(8,128)(2,1)S(1)}, bf16[1,128,8,128]{1,3,2,0:T(8,128)(2,1)}, u32[]{:S(2)}) copy-start(bf16[1,128,8,128]{1,3,2,0:T(8,128)(2,1)} %copy-done.14) | copy-start | bytes 786436
  435.0 18.6 %copy-start.21 = (bf16[1,128,1024]{2,1,0:T(8,128)(2,1)S(1)}, bf16[1,128,1024]{2,1,0:T(8,128)(2,1)}, u32[]{:S(2)}) copy-start(bf16[1,128,1024]{2,1,0:T(8,128)(2,1)} %param.8) | copy-start | bytes 786436
  451.8 18.0 %collective-permute-start.9 = (f32[1,8,128,128]{3,2,1,0:T(8,128)S(1)}, f32[1,8,128,128]{3,2,1,0:T(8,128)S(1)}, u32[]{:S(2)}, u32[]{:S(2)}) collective-permute-start(f32[1,8,128,128]{3,2,1,0:T(8,128)S(1)} %add.114), channel_id=1, source_target_pairs={{16,0},{17,1},{18,2},{19,3},{20,4},{21,5},{22,6},{23,7},{24,8},{25... | collective-permute-start | bytes 1572872 | tf_op jit(solution)/shard_map/ppermute | solution.py:19
  454.8 15.4 copy-start.11
  454.8 15.7 copy-start.3
  (3 other events, 2.6 us)
Sparse Core Ops, SparseCore 0:
  379.1 1299.9 reduce-scatter.1
